TPU v7x, 128 devices: a whole 4x4x4 slice. The times are simulated.
128 devices in a mesh: row: 16 (over y_lo, x, core), col: 8 (over z, y_hi).
Axes of the slice: x: 4, y: 4 (y_hi: 2, y_lo: 2; y = y_hi * 2 + y_lo), z: 4, core: 2. Of those that a mesh axis runs over, the one named last changes fastest.
Arguments:
- gate_feats: bfloat16 [16, 8, 1024, 256], P('row', 'col'), may hold values from -6 to 6
- adjacency: int32 [16, 8, 8, 5, 128, 128], P('row', 'col'), may hold values 0 or 1
- gate_count: int32 [16, 8], P('row', 'col'), may hold values from 128 to 1024, as said below
- membership: int32 [16, 8, 512, 1024], P('row', 'col'), may hold values 0 or 1
- tok_count: int32 [16, 8], P('row', 'col'), may hold values from 64 to 512, as said below
- w_msg: bfloat16 [256, 256], replicated, may hold values from -0.375 to 0.375
- w_query: bfloat16 [256, 256], replicated, may hold values from -0.375 to 0.375
- w_key: bfloat16 [256, 256], replicated, may hold values from -0.375 to 0.375
- w_value: bfloat16 [256, 256], replicated, may hold values from -0.375 to 0.375
- w_out: bfloat16 [256, 256], replicated, may hold values from -0.375 to 0.375
- w_score: bfloat16 [256], replicated, may hold values from -0.375 to 0.375
- cotangent: float32 [16, 8, 512], P('row', 'col'), may hold values from -6 to 6
Outputs:
- value_out: float32 [16, 8, 512], P('row', 'col')
- g_msg: float32 [256, 256], replicated
- g_query: float32 [256, 256], replicated
- g_key: float32 [256, 256], replicated
- g_value: float32 [256, 256], replicated
- g_out: float32 [256, 256], replicated
- g_score: float32 [256], replicated
Inputs may be any that keep to these rules, and one draw needn't show every extreme that they name: `gate_count`: some tile is full in every draw. `tok_count`: some tile is full in every draw.
All inputs are finite; a program needn't handle non-finite values. No bound on the sum of `adjacency` or of `membership` on one device may be relied on, other than what follows from the above.
Results may differ from a plain program's by a relative error of at most 0.017.
Values may be sent and summed in bfloat16 or wider, within the bound.
No kernel may reach another device: no remote copies, remote signals or barrier semaphores. Data moves between devices by JAX's collectives and lax.ppermute only.
A program may use at most 128 MiB of HBM per device.

v0:
```python
import math
import jax
import jax.numpy as jnp
from jax import lax
from jax.sharding import PartitionSpec as P

H = 256
HEADS = 2
HD = 128
BLK = 128
NB = 8
NT = 512
EPS = 1e-06


def with_halo(array, sides, width):
    for axis, dim in sides:
        size, length = (lax.axis_size(axis), array.shape[dim])
        up = [(i, (i + 1) % size) for i in range(size - 1)]
        down = [(j, i) for i, j in up]
        last = lax.slice_in_dim(array, length - width, length, axis=dim)
        first = lax.slice_in_dim(array, 0, width, axis=dim)
        before = lax.ppermute(last, axis, up)
        after = lax.ppermute(first, axis, down)
        array = jnp.concatenate([before, array, after], axis=dim)
    return array


def silu_grad(preact):
    sigmoid_val = jax.nn.sigmoid(preact)
    return sigmoid_val * (1.0 + preact * (1.0 - sigmoid_val))


def rms_forward(values_in):
    rscale = lax.rsqrt(jnp.mean(values_in * values_in, axis=-1, keepdims=True) + EPS)
    return (values_in * rscale, rscale)


def rms_backward(grad_in, normed, rscale):
    return rscale * (grad_in - normed * jnp.mean(grad_in * normed, axis=-1, keepdims=True))


def split_heads(rows_in):
    return rows_in.reshape(rows_in.shape[0], HEADS, HD)


def score_probs(query_rows, key_rows):
    scores = jnp.einsum(
        "qhd,khd->hqk",
        split_heads(query_rows),
        split_heads(key_rows),
        preferred_element_type=jnp.float32,
    )
    return jax.nn.sigmoid(scores / math.sqrt(HD) - math.log(NT))


def attend_sum(query_rows, key_rows, value_rows):
    weights = score_probs(query_rows, key_rows).astype(jnp.bfloat16)
    output = jnp.einsum(
        "hqk,khd->qhd", weights, split_heads(value_rows), preferred_element_type=jnp.float32
    )
    return output.reshape(query_rows.shape[0], H)


def score_grads(query_rows, grad_rows, key_rows, value_rows):
    probs_val = score_probs(query_rows, key_rows)
    grad_prob = jnp.einsum(
        "qhd,khd->hqk",
        split_heads(grad_rows),
        split_heads(value_rows),
        preferred_element_type=jnp.float32,
    )
    grad_score = (grad_prob * probs_val * (1.0 - probs_val) / math.sqrt(HD)).astype(jnp.bfloat16)
    return (probs_val.astype(jnp.bfloat16), grad_score)


def query_grad(query_rows, grad_rows, key_rows, value_rows):
    weights, grad_score = score_grads(query_rows, grad_rows, key_rows, value_rows)
    grad_query = jnp.einsum(
        "hqk,khd->qhd", grad_score, split_heads(key_rows), preferred_element_type=jnp.float32
    )
    return grad_query.reshape(query_rows.shape[0], H)


def key_value_grads(query_rows, grad_rows, key_rows, value_rows):
    weights, grad_score = score_grads(query_rows, grad_rows, key_rows, value_rows)
    grad_key = jnp.einsum(
        "hqk,qhd->khd", grad_score, split_heads(query_rows), preferred_element_type=jnp.float32
    )
    grad_val = jnp.einsum(
        "hqk,qhd->khd", weights, split_heads(grad_rows), preferred_element_type=jnp.float32
    )
    return jnp.concatenate(
        [grad_key.reshape(key_rows.shape[0], H), grad_val.reshape(key_rows.shape[0], H)], axis=1
    )


def project(rows_in, weight_mat):
    return jnp.dot(rows_in, weight_mat, preferred_element_type=jnp.float32).astype(jnp.bfloat16)


def body(
    gate_feats,
    adjacency,
    gate_count,
    membership,
    tok_count,
    w_msg,
    w_query,
    w_key,
    w_value,
    w_out,
    w_score,
    cotangent,
):
    gate_total = gate_feats.shape[2]
    gate_live = (jnp.arange(gate_total) < gate_count[0, 0]).astype(jnp.float32)
    live_feats = (gate_feats[0, 0].astype(jnp.float32) * gate_live[:, None]).astype(jnp.bfloat16)
    padded = with_halo(live_feats[None, None], (("row", 0), ("col", 1)), 1)
    sources = jnp.stack(
        [padded[1, 1], padded[0, 1], padded[2, 1], padded[1, 0], padded[1, 2]], axis=0
    )
    sources = sources.reshape(5, NB, BLK, H)
    adj_tiles = adjacency[0, 0]
    aggregate = jnp.einsum(
        "bkij,kbjh->bih",
        adj_tiles.astype(jnp.bfloat16),
        sources,
        preferred_element_type=jnp.float32,
    )
    degree = jnp.sum(adj_tiles, axis=(1, 3)).astype(jnp.float32)
    message = (aggregate / (degree[:, :, None] + 1.0)).astype(jnp.bfloat16).reshape(gate_total, H)
    preact = jnp.dot(message, w_msg, preferred_element_type=jnp.float32)
    hidden = (gate_live[:, None] * (live_feats.astype(jnp.float32) + jax.nn.silu(preact))).astype(
        jnp.bfloat16
    )
    member_rows = membership[0, 0].astype(jnp.bfloat16)
    member_count = jnp.sum(membership[0, 0], axis=1).astype(jnp.float32)[:, None]
    pooled = jnp.dot(member_rows, hidden, preferred_element_type=jnp.float32) / (member_count + 1.0)
    normed, rscale = rms_forward(pooled)
    token_live = (jnp.arange(NT) < tok_count[0, 0]).astype(jnp.float32)[:, None]
    tokens = (token_live * normed).astype(jnp.bfloat16)
    query_own = project(tokens, w_query)
    zero_rows = jnp.zeros((NT, H), jnp.float32)
    key_own = project(tokens, w_key)
    value_own = project(tokens, w_value)
    attended = attend_sum(
        query_own,
        lax.all_gather(key_own, "col", axis=0, tiled=True),
        lax.all_gather(value_own, "col", axis=0, tiled=True),
    )
    attended = attended.astype(jnp.bfloat16)
    proj = jnp.dot(attended, w_out, preferred_element_type=jnp.float32)
    pnormed, pscale = rms_forward(proj)
    mixed = tokens.astype(jnp.float32) + pnormed
    score_w = w_score.astype(jnp.float32)
    value_out = token_live[:, 0] * jnp.sum(mixed * score_w, axis=1)
    loss_weight = 1.0 / math.sqrt(lax.axis_size("row") * lax.axis_size("col") * NT)
    grad_value = token_live[:, 0] * cotangent[0, 0] * loss_weight
    g_score = jnp.sum(mixed * grad_value[:, None], axis=0)
    grad_mixed = grad_value[:, None] * score_w
    grad_proj = rms_backward(grad_mixed, pnormed, pscale).astype(jnp.bfloat16)
    g_out = jnp.einsum("nh,ne->he", attended, grad_proj, preferred_element_type=jnp.float32)
    grad_attn = jnp.dot(grad_proj, w_out.T, preferred_element_type=jnp.float32).astype(jnp.bfloat16)
    key_all, value_all = (
        lax.all_gather(key_own, "col", axis=0, tiled=True),
        lax.all_gather(value_own, "col", axis=0, tiled=True),
    )

    def add_query(running, pair_in):
        return (running + query_grad(query_own, grad_attn, pair_in[0], pair_in[1]), 0)

    grad_query, unused = lax.scan(
        add_query, zero_rows, (key_all.reshape(-1, NT, H), value_all.reshape(-1, NT, H))
    )
    key_part = key_all.reshape(lax.axis_size("col") * NT // NT, NT, H)
    value_part = value_all.reshape(lax.axis_size("col") * NT // NT, NT, H)
    terms = lax.map(
        lambda pair_in: key_value_grads(query_own, grad_attn, pair_in[0], pair_in[1]),
        (key_part, value_part),
    )
    key_sums = lax.psum_scatter(
        terms.reshape(lax.axis_size("col") * NT, 2 * H), "col", scatter_dimension=0, tiled=True
    )
    grad_query = grad_query.astype(jnp.bfloat16)
    grad_key = key_sums[:, :H].astype(jnp.bfloat16)
    grad_val = key_sums[:, H:].astype(jnp.bfloat16)
    g_query = jnp.einsum("nh,ne->he", tokens, grad_query, preferred_element_type=jnp.float32)
    g_key = jnp.einsum("nh,ne->he", tokens, grad_key, preferred_element_type=jnp.float32)
    g_value = jnp.einsum("nh,ne->he", tokens, grad_val, preferred_element_type=jnp.float32)
    grad_tokens = grad_mixed + jnp.dot(grad_query, w_query.T, preferred_element_type=jnp.float32)
    grad_tokens = grad_tokens + jnp.dot(grad_key, w_key.T, preferred_element_type=jnp.float32)
    grad_tokens = grad_tokens + jnp.dot(grad_val, w_value.T, preferred_element_type=jnp.float32)
    grad_pooled = rms_backward(token_live * grad_tokens, normed, rscale)
    grad_scaled = (grad_pooled / (member_count + 1.0)).astype(jnp.bfloat16)
    grad_hidden = jnp.einsum(
        "ng,nh->gh", member_rows, grad_scaled, preferred_element_type=jnp.float32
    )
    grad_pre = (gate_live[:, None] * grad_hidden * silu_grad(preact)).astype(jnp.bfloat16)
    g_msg = jnp.einsum("gh,ge->he", message, grad_pre, preferred_element_type=jnp.float32)
    summed = lax.psum((g_msg, g_query, g_key, g_value, g_out, g_score), ("row", "col"))
    return (value_out[None, None], summed[0], summed[1], summed[2], summed[3], summed[4], summed[5])


def solution(mesh):
    placed = (
        P("row", "col", None, None),
        P("row", "col", None, None, None, None),
        P("row", "col"),
        P("row", "col", None, None),
        P("row", "col"),
        P(),
        P(),
        P(),
        P(),
        P(),
        P(),
        P("row", "col", None),
    )
    return jax.shard_map(
        body,
        mesh=mesh,
        in_specs=placed,
        out_specs=(P("row", "col", None), P(), P(), P(), P(), P(), P()),
        check_vma=False,
    )
```

profile of v0, /device:TPU:1, one launch (start us, length us, event | category | flops | bytes accessed | tf_op | source)
XLA Modules:
  0.0 574.1 jit_solution(18341425830394711041)
XLA Ops:
  7.9 1.4 multiply_convert_fusion.3
  9.3 4.5 collective-permute-start
  13.9 1.9 collective-permute-start.1
  15.8 4.2 collective-permute-done
  20.0 4.4 collective-permute-done.1
  24.4 1.3 pad_maximum_fusion
  25.7 6.1 %collective-permute-start.2 = (bf16[3,1,1024,256]{3,2,1,0:T(8,128)(2,1)}, bf16[3,1,1024,256]{3,2,1,0:T(8,128)(2,1)}, u32[]{:S(2)}, u32[]{:S(2)}) collective-permute-start(bf16[3,1,1024,256]{3,2,1,0:T(8,128)(2,1)} %pad_maximum_fusion), channel_id=1, source_target_pairs={{0,1},{1,2},{2,3},{3,4},{4,5},{5,6},{6,7},{8,9},{9,10},{10,11},{11... | collective-permute-start | bytes 4718600 | tf_op jit(solution)/shard_map/ppermute | solution.py:23
  31.8 1.3 collective-permute-start.3
  33.3 1.8 reduce_sum.75
  37.2 21.7 %collective-permute-done.2 = bf16[3,1,1024,256]{3,2,1,0:T(8,128)(2,1)} collective-permute-done((bf16[3,1,1024,256]{3,2,1,0:T(8,128)(2,1)}, bf16[3,1,1024,256]{3,2,1,0:T(8,128)(2,1)}, u32[]{:S(2)}, u32[]{:S(2)}) %collective-permute-start.2) | collective-permute-done | bytes 1572896 | tf_op jit(solution)/shard_map/ppermute | solution.py:23
  60.1 34.4 %collective-permute-done.3 = bf16[3,1,1024,256]{3,2,1,0:T(8,128)(2,1)} collective-permute-done((bf16[3,1,1024,256]{3,2,1,0:T(8,128)(2,1)}, bf16[3,1,1024,256]{3,2,1,0:T(8,128)(2,1)}, u32[]{:S(2)}, u32[]{:S(2)}) %collective-permute-start.3) | collective-permute-done | bytes 1572896 | tf_op jit(solution)/shard_map/ppermute | solution.py:24
  101.8 58.7 %all-gather.3.cloned.1.call-done = bf16[4096,256]{1,0:T(8,128)(2,1)} async-done(((bf16[512,256]{1,0:T(8,128)(2,1)}), bf16[4096,256]{1,0:T(8,128)(2,1)}) %all-gather.3.cloned.1.call-update) | async-done | bytes 2097168 | tf_op jit(solution)/shard_map/all_gather | solution.py:150
  160.5 2.9 copy.43
  163.4 51.9 %all-gather.5.cloned.1.call-done = bf16[4096,256]{1,0:T(8,128)(2,1)} async-done(((bf16[512,256]{1,0:T(8,128)(2,1)}), bf16[4096,256]{1,0:T(8,128)(2,1)}) %all-gather.5.cloned.1.call-update) | async-done | bytes 2097168 | tf_op jit(solution)/shard_map/all_gather | solution.py:149
  215.4 4.2 copy.44
  219.5 9.6 %fusion.32 = bf16[2,128,512]{2,1,0:T(8,128)(2,1)} fusion(bf16[4096,2,128]{0,2,1:T(8,128)(2,1)S(1)} %bitcast.190, bf16[512,2,128]{0,2,1:T(8,128)(2,1)S(1)} %bitcast.182, bf16[4096,2,128]{0,2,1:T(8,128)(2,1)} %bitcast.191), kind=kOutput, calls=%fused_computation.49 | convolution fusion | flops 2172780544 | bytes 4718592 | tf_op jit(solution)/shard_map/hqk,khd->qhd/dot_general | solution.py:59
  229.2 1.4 multiply_reduce_fusion.2
  230.6 1.6 multiply_reduce_fusion
  232.7 1.8 convolution_convert_fusion
  235.6 2.4 copy.30
  238.0 52.7 %while.25 = (s32[]{:T(128)}, f32[8,512,512]{2,1,0:T(8,128)}, bf16[8,512,256]{2,1,0:T(8,128)(2,1)}, bf16[512,256]{0,1:T(8,128)(2,1)S(1)}, bf16[8,512,256]{1,2,0:T...) while((s32[]{:T(128)}, f32[8,512,512]{2,1,0:T(8,128)}, bf16[8,512,256]{2,1,0:T(8,128)(2,1)}, ...), condition=%wide.region_9.10_spmd, body=%wide.region_8.9_spmd.sunk | while | flops 542900224 | bytes 18875020 | solution.py:178
  240.9 1.7 fusion.152
  247.5 1.7 fusion.152
  254.1 1.7 fusion.152
  260.6 1.7 fusion.152
  267.2 1.7 fusion.152
  273.8 1.7 fusion.152
  280.4 1.7 fusion.152
  286.9 1.7 fusion.152
  289.5 1.1 constant_dynamic-update-slice_fusion.6
  291.8 53.8 %while.26 = (s32[]{:T(128)}, f32[512,256]{0,1:T(8,128)S(1)}, bf16[8,512,256]{1,2,0:T(8,128)(2,1)}, bf16[8,512,256]{2,1,0:T(8,128)(2,1)}, bf16[512,256]{1,0:T(8,1...) while((s32[]{:T(128)}, f32[512,256]{0,1:T(8,128)S(1)}, ...), condition=%wide.region_7.8_spmd.clone, body=%wide.region_6.7_spmd.clone.sunk | while | flops 408158208 | bytes 9437287 | solution.py:173
  294.4 1.7 constant_dynamic-slice_fusion.10
  296.1 2.3 fusion.160
  301.1 1.7 constant_dynamic-slice_fusion.10
  302.8 2.3 fusion.160
  306.3 1.1 copy.74
  307.8 1.7 constant_dynamic-slice_fusion.10
  309.5 2.3 fusion.160
  314.5 1.7 constant_dynamic-slice_fusion.10
  316.2 2.3 fusion.160
  319.7 1.1 copy.74
  321.3 1.7 constant_dynamic-slice_fusion.10
  322.9 2.3 fusion.160
  326.5 1.1 copy.74
  328.0 1.7 constant_dynamic-slice_fusion.10
  329.7 2.3 fusion.160
  333.3 1.1 copy.74
  334.8 1.7 constant_dynamic-slice_fusion.10
  336.5 2.3 fusion.160
  340.0 1.1 copy.74
  341.5 1.7 constant_dynamic-slice_fusion.10
  343.2 2.3 fusion.160
  346.6 2.1 fusion.91
  348.8 53.9 %reduce-scatter.2.cloned.1.call-done = f32[512,512]{1,0:T(8,128)} async-done(((f32[4096,512]{1,0:T(8,128)}), f32[512,512]{1,0:T(8,128)}) %reduce-scatter.2.cloned.1.call-update) | async-done | bytes 1048592 | tf_op jit(solution)/shard_map/reduce_scatter | solution.py:182
  402.7 1.3 convert.6
  405.9 1.3 fusion.74
  407.6 1.1 fusion.49
  408.7 3.2 fusion.28
  412.0 65.1 %psum.47 = f32[256]{0:T(256)} all-reduce(f32[256]{0:T(256)S(1)} %copy-done.29), channel_id=1, replica_groups=mesh['row'=16,'col'=8] {'row','col'}, use_global_device_ids=true, to_apply=%region_18.19 | all-reduce | flops 256 | bytes 2048 | tf_op jit(solution)/shard_map/psum | solution.py:201
  477.6 82.6 %all-reduce.3.cloned.1.call-done = (f32[256,256]{1,0:T(8,128)}, f32[256,256]{1,0:T(8,128)}, f32[256,256]{1,0:T(8,128)}, f32[256,256]{1,0:T(8,128)}, f32[256,256]{1,0:T(8,128)}) async-done(((f32[256,256]{1,0:T(8,128)}, f32[256,256]{1,0:T(8,128)}, f32[256,256]{1,0:T(8,128)}, f32[256,256]{1,0:T(8,128)}, f32[256,256]{1,0:T(8,128)}), (f32[256,256]{1,0:T(8,128)}, f32[256,256]{1,0:T(8,128)}, f32[256,256]{1,0:T(8,128)}, ...) | async-done | bytes 1310736 | tf_op jit(solution)/shard_map/psum | solution.py:201
  560.2 1.7 copy.99
  561.9 1.7 copy.100
  563.6 1.7 copy.101
  565.2 1.7 copy.102
  (238 shorter events, 70.9 us)
Async XLA Ops:
  7.2 222.0 %copy-start = (bf16[256,256]{1,0:T(8,128)(2,1)S(1)}, bf16[256,256]{1,0:T(8,128)(2,1)}, u32[]{:S(2)}) copy-start(bf16[256,256]{1,0:T(8,128)(2,1)} %param.25) | copy-start | bytes 393220
  7.2 153.3 %all-gather.3.cloned.1.call-start = ((), (), s32[]{:S(2)}) async-start(), calls=%async_computation.1 | async-start | bytes 2359296 | tf_op jit(solution)/shard_map/all_gather | solution.py:150
  7.9 88.9 %copy-start.24 = (f32[1024]{0:T(1024)}, f32[1024]{0:T(1024)S(1)}, u32[]{:S(2)}) copy-start(f32[1024]{0:T(1024)S(1)} %fusion.84) | copy-start | bytes 12292
  7.9 25.2 %copy-start.7 = (s32[1,1,8,5,128,128]{5,4,3,2,1,0:T(8,128)S(1)}, s32[1,1,8,5,128,128]{5,4,3,2,1,0:T(8,128)}, u32[]{:S(2)}) copy-start(s32[1,1,8,5,128,128]{5,4,3,2,1,0:T(8,128)} %param.17) | copy-start | bytes 7864324
  9.3 10.6 %collective-permute-start = (bf16[1,1,1024,256]{3,2,1,0:T(8,128)(2,1)S(1)}, bf16[1,1,1024,256]{3,2,1,0:T(8,128)(2,1)S(1)}, u32[]{:S(2)}, u32[]{:S(2)}) collective-permute-start(bf16[1,1,1024,256]{3,2,1,0:T(8,128)(2,1)S(1)} %multiply_convert_fusion.3), channel_id=1, source_target_pairs={{0,8},{8,16},{16,24},{24,32},{32,40},{40,48},{48,56},{56,64},{64,7... | collective-permute-start | bytes 1572872 | tf_op jit(solution)/shard_map/ppermute | solution.py:23
  13.9 10.5 %collective-permute-start.1 = (bf16[1,1,1024,256]{3,2,1,0:T(8,128)(2,1)S(1)}, bf16[1,1,1024,256]{3,2,1,0:T(8,128)(2,1)S(1)}, u32[]{:S(2)}, u32[]{:S(2)}) collective-permute-start(bf16[1,1,1024,256]{3,2,1,0:T(8,128)(2,1)S(1)} %multiply_convert_fusion.3), channel_id=1, source_target_pairs={{8,0},{16,8},{24,16},{32,24},{40,32},{48,40},{56,48},{64,56},{72,6... | collective-permute-start | bytes 1572872 | tf_op jit(solution)/shard_map/ppermute | solution.py:24
  20.0 4.4 copy-start.12
  24.4 1.3 copy-start.13
  25.7 10.2 %copy-start.10 = (bf16[1,1,1024,256]{3,2,1,0:T(8,128)(2,1)S(1)}, bf16[1,1,1024,256]{3,2,1,0:T(8,128)(2,1)}, u32[]{:S(2)}) copy-start(bf16[1,1,1024,256]{3,2,1,0:T(8,128)(2,1)} %param.16) | copy-start | bytes 1572868
  25.7 33.2 %collective-permute-start.2 = (bf16[3,1,1024,256]{3,2,1,0:T(8,128)(2,1)}, bf16[3,1,1024,256]{3,2,1,0:T(8,128)(2,1)}, u32[]{:S(2)}, u32[]{:S(2)}) collective-permute-start(bf16[3,1,1024,256]{3,2,1,0:T(8,128)(2,1)} %pad_maximum_fusion), channel_id=1, source_target_pairs={{0,1},{1,2},{2,3},{3,4},{4,5},{5,6},{6,7},{8,9},{9,10},{10,11},{11... | collective-permute-start | bytes 4718600 | tf_op jit(solution)/shard_map/ppermute | solution.py:23
  31.8 62.7 %collective-permute-start.3 = (bf16[3,1,1024,256]{3,2,1,0:T(8,128)(2,1)}, bf16[3,1,1024,256]{3,2,1,0:T(8,128)(2,1)}, u32[]{:S(2)}, u32[]{:S(2)}) collective-permute-start(bf16[3,1,1024,256]{3,2,1,0:T(8,128)(2,1)} %pad_maximum_fusion), channel_id=1, source_target_pairs={{1,0},{2,1},{3,2},{4,3},{5,4},{6,5},{7,6},{9,8},{10,9},{11,10},{12... | collective-permute-start | bytes 4718600 | tf_op jit(solution)/shard_map/ppermute | solution.py:24
  35.1 2.1 copy-start.14
  35.9 61.0 %copy-start.31 = (f32[512]{0:T(512)}, f32[512]{0:T(512)S(1)}, u32[]{:S(2)}) copy-start(f32[512]{0:T(512)S(1)} %convert_add_fusion.2) | copy-start | bytes 6148
  95.6 0.9 copy-start.23
  95.6 1.7 copy-start.8
  95.6 1.9 copy-start.11
  96.3 2.1 copy-start.21
  97.6 1.0 copy-start.15
  97.6 1.1 copy-start.16
  97.6 2.2 copy-start.17
  98.6 132.0 %copy-start.4 = (f32[256,512]{1,0:T(8,128)}, f32[256,512]{1,0:T(8,128)S(1)}, u32[]{:S(2)}) copy-start(f32[256,512]{1,0:T(8,128)S(1)} %get-tuple-element.241) | copy-start | bytes 1572868
  98.6 2.4 copy-start.33
  98.6 3.0 copy-start.30
  98.6 3.0 copy-start.19
  99.7 115.7 %all-gather.5.cloned.1.call-start = ((), (), s32[]{:S(2)}) async-start(), calls=%async_computation.2 | async-start | bytes 2359296 | tf_op jit(solution)/shard_map/all_gather | solution.py:149
  100.7 302.0 %reduce-scatter.2.cloned.1.call-start = ((), (), s32[]{:S(2)}) async-start(), calls=%async_computation.3 | async-start | bytes 9437184 | tf_op jit(solution)/shard_map/reduce_scatter | solution.py:182
  229.1 6.4 %copy-start.3 = (bf16[4096,256]{1,0:T(8,128)(2,1)S(1)}, bf16[4096,256]{1,0:T(8,128)(2,1)}, u32[]{:S(2)}) copy-start(bf16[4096,256]{1,0:T(8,128)(2,1)} %all-gather.5.cloned.1.call-done) | copy-start | bytes 6291460
  230.5 1.6 copy-start.6
  232.1 0.6 copy-start.28
  238.0 1.8 copy-start.1
  243.2 1.4 copy-start.2
  244.6 1.8 copy-start.1
  249.8 1.4 copy-start.2
  251.2 1.8 copy-start.1
  256.3 1.4 copy-start.2
  257.7 1.8 copy-start.1
  262.9 1.4 copy-start.2
  264.3 1.8 copy-start.1
  269.5 1.4 copy-start.2
  270.9 1.8 copy-start.1
  276.0 1.4 copy-start.2
  277.5 1.8 copy-start.1
  282.6 1.4 copy-start.2
  284.0 1.8 copy-start.1
  289.2 1.5 copy-start.2
  290.7 269.5 %all-reduce.3.cloned.1.call-start = ((), (), s32[]{:S(2)}) async-start(), calls=%async_computation.4 | async-start | bytes 2621440 | tf_op jit(solution)/shard_map/psum | solution.py:201
  348.8 58.7 %copy-start.5 = (f32[256,512]{1,0:T(8,128)S(1)}, f32[256,512]{1,0:T(8,128)}, u32[]{:S(2)}) copy-start(f32[256,512]{1,0:T(8,128)} %copy-done.4) | copy-start | bytes 1572868
  348.8 58.7 %copy-start.26 = (f32[256]{0:T(256)S(1)}, f32[256]{0:T(256)}, u32[]{:S(2)}) copy-start(f32[256]{0:T(256)} %convert_element_type.188) | copy-start | bytes 3076
  402.7 4.5 copy-start.18
  402.7 4.8 copy-start.20
  405.9 2.7 copy-start.9
  405.9 2.7 copy-start.25
  405.9 2.7 copy-start.32
  408.7 3.3 copy-start.29
  408.7 68.3 %copy-start.27 = (f32[512]{0:T(512)S(1)}, f32[512]{0:T(512)}, u32[]{:S(2)}) copy-start(f32[512]{0:T(512)} %get-tuple-element.209) | copy-start | bytes 6148
  560.2 6.7 %copy-start.22 = (f32[256,256]{1,0:T(8,128)S(1)}, f32[256,256]{1,0:T(8,128)}, u32[]{:S(2)}) copy-start(f32[256,256]{1,0:T(8,128)} %get-tuple-element.370) | copy-start | bytes 786436
Sparse Core Ops, SparseCore 0:
  99.8 60.6 all-gather.2
  163.4 51.8 all-gather.4
  290.8 111.8 reduce-scatter.1
  412.1 148.0 all-reduce.2
where the time goes:
time: 577 us; the launch traced here: 574 us
  waiting for transfers between devices  312 us (54%)
  local copies, waits for them, and re-layouts  82.6 us (14%)
  matrix products  72.8 us (13%)
  blocking collectives  65.1 us (11%)
  between operations  15.6 us (3%)
  starting transfers between devices  14.4 us (2%)
  other arithmetic  10.9 us (2%)
    psum x1, waiting for transfers between devices, body(): lax.psum((g_msg, g_query, g_key, g_value, g_out, g_score), ('row', 'col'))  82.6 us
    psum x1, blocking collectives, body(): lax.psum((g_msg, g_query, g_key, g_value, g_out, g_score), ('row', 'col'))  65.1 us
    all_gather x1, waiting for transfers between devices, body(): lax.all_gather(value_own, 'col', axis=0, tiled=True)  58.7 us
    reduce_scatter x1, waiting for transfers between devices, body(): lax.psum_scatter(terms.reshape(lax.axis_size('col') * NT, 2 * H), 'col',...  53.9 us
    all_gather x1, waiting for transfers between devices, body(): lax.all_gather(key_own, 'col', axis=0, tiled=True)  51.9 us
    ppermute x2, waiting for transfers between devices, with_halo(): after = lax.ppermute(first, axis, down)  38.8 us
    dynamic_slice x32, local copies, waits for them, and re-layouts, body(): lax.scan(add_query, zero_rows, (key_all.reshape(-1, NT, H), value_all.res...  37.6 us
    ppermute x2, waiting for transfers between devices, with_halo(): before = lax.ppermute(last, axis, up)  25.9 us
  transfers between devices with their start and end apart: 8, of which 8 were waited for; matrix products, arithmetic and copies ran while one was open for 12% of the time, Pallas kernels for 0%

commit v1 on v0

--- a/solution.py
+++ b/solution.py
@@ -198,7 +198,7 @@
     )
     grad_pre = (gate_live[:, None] * grad_hidden * silu_grad(preact)).astype(jnp.bfloat16)
     g_msg = jnp.einsum("gh,ge->he", message, grad_pre, preferred_element_type=jnp.float32)
-    summed = lax.psum((g_msg, g_query, g_key, g_value, g_out, g_score), ("row", "col"))
+    summed = lax.psum(lax.psum((g_msg, g_query, g_key, g_value, g_out, g_score), "col"), "row")
     return (value_out[None, None], summed[0], summed[1], summed[2], summed[3], summed[4], summed[5])
 
 

time: 577 us -> 643 us (1.11)
  waiting for transfers between devices: 312 us -> 390 us
  blocking collectives: 65.1 us -> 53.5 us
    psum x1 -> x2, waiting for transfers between devices: 82.6 us -> 161 us  [the longest x1 88.7 us: body(): lax.psum((g_msg, g_query, g_key, g_value, g_out, g_score), 'col')]
    psum x1 -> x2, blocking collectives: 65.1 us -> 53.5 us  [the longest x1 35 us: body(): lax.psum(lax.psum((g_msg, g_query, g_key, g_value, g_out, g_score), 'col'...]
  transfers between devices with their start and end apart: 8 -> 9, of which waited for: 8 -> 9; matrix products, arithmetic and copies ran while one was open for 12% -> 11% of each run, Pallas kernels for 0% -> 0%
where the time goes in v1:
time: 643 us; the launch traced here: 641 us
  waiting for transfers between devices  390 us (61%)
  local copies, waits for them, and re-layouts  82.5 us (13%)
  matrix products  72.9 us (11%)
  blocking collectives  53.5 us (8%)
  between operations  15.6 us (2%)
  starting transfers between devices  14.4 us (2%)
  other arithmetic  10.9 us (2%)
    psum x1, waiting for transfers between devices, body(): lax.psum((g_msg, g_query, g_key, g_value, g_out, g_score), 'col')  88.7 us
    psum x1, waiting for transfers between devices, body(): lax.psum(lax.psum((g_msg, g_query, g_key, g_value, g_out, g_score), 'col'...  72.1 us
    all_gather x1, waiting for transfers between devices, body(): lax.all_gather(value_own, 'col', axis=0, tiled=True)  58.7 us
    reduce_scatter x1, waiting for transfers between devices, body(): lax.psum_scatter(terms.reshape(lax.axis_size('col') * NT, 2 * H), 'col',...  53.8 us
    all_gather x1, waiting for transfers between devices, body(): lax.all_gather(key_own, 'col', axis=0, tiled=True)  51.9 us
    ppermute x2, waiting for transfers between devices, with_halo(): after = lax.ppermute(first, axis, down)  38.8 us
    dynamic_slice x32, local copies, waits for them, and re-layouts, body(): lax.scan(add_query, zero_rows, (key_all.reshape(-1, NT, H), value_all.res...  37.5 us
    psum x1, blocking collectives, body(): lax.psum(lax.psum((g_msg, g_query, g_key, g_value, g_out, g_score), 'col'...  35 us
  transfers between devices with their start and end apart: 9, of which 9 were waited for; matrix products, arithmetic and copies ran while one was open for 11% of the time, Pallas kernels for 0%

profile of v1, /device:TPU:1, one launch (start us, length us, event | category | flops | bytes accessed | tf_op | source)
XLA Modules:
  0.0 640.9 jit_solution(5606768925575048924)
XLA Ops:
  7.9 1.4 multiply_convert_fusion.3
  9.3 4.5 collective-permute-start
  13.9 1.9 collective-permute-start.1
  15.8 4.2 collective-permute-done
  20.0 4.4 collective-permute-done.1
  24.4 1.3 pad_maximum_fusion
  25.7 6.1 collective-permute-start.2
  31.8 1.3 collective-permute-start.3
  33.3 1.8 reduce_sum.75
  37.2 21.7 %collective-permute-done.2 = bf16[3,1,1024,256]{3,2,1,0:T(8,128)(2,1)} collective-permute-done((bf16[3,1,1024,256]{3,2,1,0:T(8,128)(2,1)}, bf16[3,1,1024,256]{3,2,1,0:T(8,128)(2,1)}, u32[]{:S(2)}, u32[]{:S(2)}) %collective-permute-start.2) | collective-permute-done | bytes 1572896 | tf_op jit(solution)/shard_map/ppermute | solution.py:23
  60.1 34.4 %collective-permute-done.3 = bf16[3,1,1024,256]{3,2,1,0:T(8,128)(2,1)} collective-permute-done((bf16[3,1,1024,256]{3,2,1,0:T(8,128)(2,1)}, bf16[3,1,1024,256]{3,2,1,0:T(8,128)(2,1)}, u32[]{:S(2)}, u32[]{:S(2)}) %collective-permute-start.3) | collective-permute-done | bytes 1572896 | tf_op jit(solution)/shard_map/ppermute | solution.py:24
  101.8 58.7 %all-gather.3.cloned.1.call-done = bf16[4096,256]{1,0:T(8,128)(2,1)} async-done(((bf16[512,256]{1,0:T(8,128)(2,1)}), bf16[4096,256]{1,0:T(8,128)(2,1)}) %all-gather.3.cloned.1.call-update) | async-done | bytes 2097168 | tf_op jit(solution)/shard_map/all_gather | solution.py:150
  160.5 2.9 copy.43
  163.4 51.9 %all-gather.5.cloned.1.call-done = bf16[4096,256]{1,0:T(8,128)(2,1)} async-done(((bf16[512,256]{1,0:T(8,128)(2,1)}), bf16[4096,256]{1,0:T(8,128)(2,1)}) %all-gather.5.cloned.1.call-update) | async-done | bytes 2097168 | tf_op jit(solution)/shard_map/all_gather | solution.py:149
  215.3 4.1 copy.44
  219.5 9.6 %fusion.32 = bf16[2,128,512]{2,1,0:T(8,128)(2,1)} fusion(bf16[4096,2,128]{0,2,1:T(8,128)(2,1)S(1)} %bitcast.190, bf16[512,2,128]{0,2,1:T(8,128)(2,1)S(1)} %bitcast.182, bf16[4096,2,128]{0,2,1:T(8,128)(2,1)} %bitcast.191), kind=kOutput, calls=%fused_computation.49 | convolution fusion | flops 2172780544 | bytes 4718592 | tf_op jit(solution)/shard_map/hqk,khd->qhd/dot_general | solution.py:59
  229.1 1.4 multiply_reduce_fusion.2
  230.5 1.6 multiply_reduce_fusion
  232.6 1.8 convolution_convert_fusion
  235.5 2.4 copy.30
  237.9 52.7 %while.25 = (s32[]{:T(128)}, f32[8,512,512]{2,1,0:T(8,128)}, bf16[8,512,256]{2,1,0:T(8,128)(2,1)}, bf16[512,256]{0,1:T(8,128)(2,1)S(1)}, bf16[8,512,256]{1,2,0:T...) while((s32[]{:T(128)}, f32[8,512,512]{2,1,0:T(8,128)}, bf16[8,512,256]{2,1,0:T(8,128)(2,1)}, ...), condition=%wide.region_9.10_spmd, body=%wide.region_8.9_spmd.sunk | while | flops 542900224 | bytes 18875020 | solution.py:178
  240.8 1.7 fusion.152
  247.4 1.7 fusion.152
  254.0 1.7 fusion.152
  260.5 1.7 fusion.152
  267.1 1.7 fusion.152
  273.7 1.7 fusion.152
  280.3 1.7 fusion.152
  286.8 1.7 fusion.152
  289.5 1.1 constant_dynamic-update-slice_fusion.6
  291.7 54.0 %while.26 = (s32[]{:T(128)}, f32[512,256]{0,1:T(8,128)S(1)}, bf16[8,512,256]{1,2,0:T(8,128)(2,1)}, bf16[8,512,256]{2,1,0:T(8,128)(2,1)}, bf16[512,256]{1,0:T(8,1...) while((s32[]{:T(128)}, f32[512,256]{0,1:T(8,128)S(1)}, ...), condition=%wide.region_7.8_spmd.clone, body=%wide.region_6.7_spmd.clone.sunk | while | flops 408158208 | bytes 9437287 | solution.py:173
  294.3 1.7 constant_dynamic-slice_fusion.10
  296.0 2.3 fusion.160
  301.1 1.7 constant_dynamic-slice_fusion.10
  302.7 2.3 fusion.160
  307.8 1.7 constant_dynamic-slice_fusion.10
  309.5 2.3 fusion.160
  314.5 1.7 constant_dynamic-slice_fusion.10
  316.2 2.3 fusion.160
  319.7 1.1 copy.74
  321.3 1.7 constant_dynamic-slice_fusion.10
  323.0 2.3 fusion.160
  328.1 1.7 constant_dynamic-slice_fusion.10
  329.7 2.3 fusion.160
  333.3 1.1 copy.74
  334.8 1.7 constant_dynamic-slice_fusion.10
  336.5 2.3 fusion.160
  340.1 1.1 copy.74
  341.6 1.7 constant_dynamic-slice_fusion.10
  343.3 2.3 fusion.160
  346.7 2.1 fusion.91
  348.9 53.8 %reduce-scatter.2.cloned.1.call-done = f32[512,512]{1,0:T(8,128)} async-done(((f32[4096,512]{1,0:T(8,128)}), f32[512,512]{1,0:T(8,128)}) %reduce-scatter.2.cloned.1.call-update) | async-done | bytes 1048592 | tf_op jit(solution)/shard_map/reduce_scatter | solution.py:182
  402.7 1.3 convert.6
  405.9 1.3 fusion.74
  407.5 1.1 fusion.49
  408.6 3.2 fusion.28
  411.9 88.7 %all-reduce.7.cloned.1.call-done = (f32[256,256]{1,0:T(8,128)}, f32[256,256]{1,0:T(8,128)}, f32[256,256]{1,0:T(8,128)}, f32[256,256]{1,0:T(8,128)}, f32[256,256]{1,0:T(8,128)}) async-done(((f32[256,256]{1,0:T(8,128)}, f32[256,256]{1,0:T(8,128)}, f32[256,256]{1,0:T(8,128)}, f32[256,256]{1,0:T(8,128)}, f32[256,256]{1,0:T(8,128)}), (f32[256,256]{1,0:T(8,128)}, f32[256,256]{1,0:T(8,128)}, f32[256,256]{1,0:T(8,128)}, ...) | async-done | bytes 1310736 | tf_op jit(solution)/shard_map/psum | solution.py:201
  500.7 18.5 %psum.94 = f32[256]{0:T(256)S(1)} all-reduce(f32[256]{0:T(256)S(1)} %copy-done.29), channel_id=1, replica_groups=mesh['row'=16,'col'=8] {'col'}, use_global_device_ids=true, to_apply=%region_23.24 | all-reduce | flops 256 | bytes 2048 | tf_op jit(solution)/shard_map/psum | solution.py:201
  519.1 35.0 %psum.95 = f32[256]{0:T(256)} all-reduce(f32[256]{0:T(256)S(1)} %psum.94), channel_id=1, replica_groups=mesh['row'=16,'col'=8] {'row'}, use_global_device_ids=true, to_apply=%region_24.25 | all-reduce | flops 256 | bytes 2048 | tf_op jit(solution)/shard_map/psum | solution.py:201
  554.7 72.1 %all-reduce.5.cloned.1.call-done = (f32[256,256]{1,0:T(8,128)}, f32[256,256]{1,0:T(8,128)}, f32[256,256]{1,0:T(8,128)}, f32[256,256]{1,0:T(8,128)}, f32[256,256]{1,0:T(8,128)}) async-done(((f32[256,256]{1,0:T(8,128)}, f32[256,256]{1,0:T(8,128)}, f32[256,256]{1,0:T(8,128)}, f32[256,256]{1,0:T(8,128)}, f32[256,256]{1,0:T(8,128)}), (f32[256,256]{1,0:T(8,128)}, f32[256,256]{1,0:T(8,128)}, f32[256,256]{1,0:T(8,128)}, ...) | async-done | bytes 1310736 | tf_op jit(solution)/shard_map/psum | solution.py:201
  626.9 1.7 copy.104
  628.6 1.7 copy.105
  630.3 1.7 copy.106
  631.9 1.7 copy.107
  (242 shorter events, 73.1 us)
Async XLA Ops:
  7.2 221.9 %copy-start = (bf16[256,256]{1,0:T(8,128)(2,1)S(1)}, bf16[256,256]{1,0:T(8,128)(2,1)}, u32[]{:S(2)}) copy-start(bf16[256,256]{1,0:T(8,128)(2,1)} %param.25) | copy-start | bytes 393220
  7.2 153.3 %all-gather.3.cloned.1.call-start = ((), (), s32[]{:S(2)}) async-start(), calls=%async_computation.1 | async-start | bytes 2359296 | tf_op jit(solution)/shard_map/all_gather | solution.py:150
  7.9 88.9 %copy-start.24 = (f32[1024]{0:T(1024)}, f32[1024]{0:T(1024)S(1)}, u32[]{:S(2)}) copy-start(f32[1024]{0:T(1024)S(1)} %fusion.84) | copy-start | bytes 12292
  7.9 25.2 %copy-start.7 = (s32[1,1,8,5,128,128]{5,4,3,2,1,0:T(8,128)S(1)}, s32[1,1,8,5,128,128]{5,4,3,2,1,0:T(8,128)}, u32[]{:S(2)}) copy-start(s32[1,1,8,5,128,128]{5,4,3,2,1,0:T(8,128)} %param.17) | copy-start | bytes 7864324
  9.3 10.6 %collective-permute-start = (bf16[1,1,1024,256]{3,2,1,0:T(8,128)(2,1)S(1)}, bf16[1,1,1024,256]{3,2,1,0:T(8,128)(2,1)S(1)}, u32[]{:S(2)}, u32[]{:S(2)}) collective-permute-start(bf16[1,1,1024,256]{3,2,1,0:T(8,128)(2,1)S(1)} %multiply_convert_fusion.3), channel_id=1, source_target_pairs={{0,8},{8,16},{16,24},{24,32},{32,40},{40,48},{48,56},{56,64},{64,7... | collective-permute-start | bytes 1572872 | tf_op jit(solution)/shard_map/ppermute | solution.py:23
  13.9 10.5 %collective-permute-start.1 = (bf16[1,1,1024,256]{3,2,1,0:T(8,128)(2,1)S(1)}, bf16[1,1,1024,256]{3,2,1,0:T(8,128)(2,1)S(1)}, u32[]{:S(2)}, u32[]{:S(2)}) collective-permute-start(bf16[1,1,1024,256]{3,2,1,0:T(8,128)(2,1)S(1)} %multiply_convert_fusion.3), channel_id=1, source_target_pairs={{8,0},{16,8},{24,16},{32,24},{40,32},{48,40},{56,48},{64,56},{72,6... | collective-permute-start | bytes 1572872 | tf_op jit(solution)/shard_map/ppermute | solution.py:24
  20.0 4.4 copy-start.12
  24.4 1.3 copy-start.13
  25.7 10.2 %copy-start.10 = (bf16[1,1,1024,256]{3,2,1,0:T(8,128)(2,1)S(1)}, bf16[1,1,1024,256]{3,2,1,0:T(8,128)(2,1)}, u32[]{:S(2)}) copy-start(bf16[1,1,1024,256]{3,2,1,0:T(8,128)(2,1)} %param.16) | copy-start | bytes 1572868
  25.7 33.2 %collective-permute-start.2 = (bf16[3,1,1024,256]{3,2,1,0:T(8,128)(2,1)}, bf16[3,1,1024,256]{3,2,1,0:T(8,128)(2,1)}, u32[]{:S(2)}, u32[]{:S(2)}) collective-permute-start(bf16[3,1,1024,256]{3,2,1,0:T(8,128)(2,1)} %pad_maximum_fusion), channel_id=1, source_target_pairs={{0,1},{1,2},{2,3},{3,4},{4,5},{5,6},{6,7},{8,9},{9,10},{10,11},{11... | collective-permute-start | bytes 4718600 | tf_op jit(solution)/shard_map/ppermute | solution.py:23
  31.8 62.7 %collective-permute-start.3 = (bf16[3,1,1024,256]{3,2,1,0:T(8,128)(2,1)}, bf16[3,1,1024,256]{3,2,1,0:T(8,128)(2,1)}, u32[]{:S(2)}, u32[]{:S(2)}) collective-permute-start(bf16[3,1,1024,256]{3,2,1,0:T(8,128)(2,1)} %pad_maximum_fusion), channel_id=1, source_target_pairs={{1,0},{2,1},{3,2},{4,3},{5,4},{6,5},{7,6},{9,8},{10,9},{11,10},{12... | collective-permute-start | bytes 4718600 | tf_op jit(solution)/shard_map/ppermute | solution.py:24
  35.1 2.1 copy-start.14
  35.8 61.0 %copy-start.31 = (f32[512]{0:T(512)}, f32[512]{0:T(512)S(1)}, u32[]{:S(2)}) copy-start(f32[512]{0:T(512)S(1)} %convert_add_fusion.2) | copy-start | bytes 6148
  95.6 0.9 copy-start.23
  95.6 1.7 copy-start.8
  95.6 1.9 copy-start.11
  96.3 2.1 copy-start.21
  97.6 1.0 copy-start.15
  97.6 1.1 copy-start.16
  97.6 2.1 copy-start.17
  98.5 131.9 %copy-start.4 = (f32[256,512]{1,0:T(8,128)}, f32[256,512]{1,0:T(8,128)S(1)}, u32[]{:S(2)}) copy-start(f32[256,512]{1,0:T(8,128)S(1)} %get-tuple-element.246) | copy-start | bytes 1572868
  98.5 2.4 copy-start.33
  98.6 3.0 copy-start.30
  98.6 3.0 copy-start.19
  99.6 115.7 %all-gather.5.cloned.1.call-start = ((), (), s32[]{:S(2)}) async-start(), calls=%async_computation.2 | async-start | bytes 2359296 | tf_op jit(solution)/shard_map/all_gather | solution.py:149
  100.7 301.9 %reduce-scatter.2.cloned.1.call-start = ((), (), s32[]{:S(2)}) async-start(), calls=%async_computation.3 | async-start | bytes 9437184 | tf_op jit(solution)/shard_map/reduce_scatter | solution.py:182
  229.1 6.4 %copy-start.3 = (bf16[4096,256]{1,0:T(8,128)(2,1)S(1)}, bf16[4096,256]{1,0:T(8,128)(2,1)}, u32[]{:S(2)}) copy-start(bf16[4096,256]{1,0:T(8,128)(2,1)} %all-gather.5.cloned.1.call-done) | copy-start | bytes 6291460
  230.5 1.6 copy-start.6
  232.0 0.6 copy-start.28
  237.9 1.8 copy-start.1
  243.1 1.4 copy-start.2
  244.5 1.8 copy-start.1
  249.7 1.4 copy-start.2
  251.1 1.8 copy-start.1
  256.2 1.4 copy-start.2
  257.6 1.8 copy-start.1
  262.8 1.4 copy-start.2
  264.2 1.8 copy-start.1
  269.4 1.4 copy-start.2
  270.8 1.8 copy-start.1
  276.0 1.4 copy-start.2
  277.4 1.8 copy-start.1
  282.6 1.4 copy-start.2
  284.0 1.8 copy-start.1
  289.1 1.5 copy-start.2
  290.6 210.0 %all-reduce.7.cloned.1.call-start = ((), (), s32[]{:S(2)}) async-start(), calls=%async_computation.5 | async-start | bytes 2621440 | tf_op jit(solution)/shard_map/psum | solution.py:201
  348.9 58.6 %copy-start.5 = (f32[256,512]{1,0:T(8,128)S(1)}, f32[256,512]{1,0:T(8,128)}, u32[]{:S(2)}) copy-start(f32[256,512]{1,0:T(8,128)} %copy-done.4) | copy-start | bytes 1572868
  348.9 58.6 %copy-start.26 = (f32[256]{0:T(256)S(1)}, f32[256]{0:T(256)}, u32[]{:S(2)}) copy-start(f32[256]{0:T(256)} %convert_element_type.188) | copy-start | bytes 3076
  402.7 4.5 copy-start.18
  402.7 4.8 copy-start.20
  405.9 2.7 copy-start.9
  405.9 2.7 copy-start.25
  405.9 2.7 copy-start.32
  411.9 88.8 %copy-start.29 = (f32[256]{0:T(256)S(1)}, f32[256]{0:T(256)}, u32[]{:S(2)}) copy-start(f32[256]{0:T(256)} %get-tuple-element.208) | copy-start | bytes 3076
  411.9 142.3 %copy-start.27 = (f32[512]{0:T(512)S(1)}, f32[512]{0:T(512)}, u32[]{:S(2)}) copy-start(f32[512]{0:T(512)} %get-tuple-element.209) | copy-start | bytes 6148
  411.9 215.0 %all-reduce.5.cloned.1.call-start = ((), (), s32[]{:S(2)}) async-start(), calls=%async_computation.4 | async-start | bytes 2621440 | tf_op jit(solution)/shard_map/psum | solution.py:201
  626.9 6.7 %copy-start.22 = (f32[256,256]{1,0:T(8,128)S(1)}, f32[256,256]{1,0:T(8,128)}, u32[]{:S(2)}) copy-start(f32[256,256]{1,0:T(8,128)} %get-tuple-element.375) | copy-start | bytes 786436
Sparse Core Ops, SparseCore 0:
  99.8 60.6 all-gather.2
  163.4 51.8 all-gather.4
  290.7 111.8 reduce-scatter.1
  412.0 88.5 all-reduce.6
  503.6 123.2 all-reduce.4
